TPU v7x, 256 devices: a whole 4x4x8 slice. The times are simulated.
256 devices in a mesh: section: 4 (over x), seq: 16 (over z, y_hi), tp: 4 (over y_lo, core).
Axes of the slice: x: 4, y: 4 (y_hi: 2, y_lo: 2; y = y_hi * 2 + y_lo), z: 8, core: 2. Of those that a mesh axis runs over, the one named last changes fastest.
Arguments:
- queries: bfloat16 [4, 4096, 8192], P('section', 'seq', 'tp'), may hold values from -135 to 135
- upstream: bfloat16 [4, 4096, 8192], P('section', 'seq', 'tp'), may hold values from -48 to 48
- shared_kv: bfloat16 [2, 4096, 1024], P(None, ('seq', 'tp')), may hold values from -5 to 5
Outputs:
- d_queries: bfloat16 [4, 4096, 8192], P('section', 'seq', 'tp')
- d_shared_kv: float32 [2, 4096, 1024], P(None, ('seq', 'tp'))
All inputs are finite; a program needn't handle non-finite values.
Results may differ from a plain program's by a relative error of at most 0.0098.
Values may be sent and summed in bfloat16 or wider, within the bound.
No kernel may reach another device: no remote copies, remote signals or barrier semaphores. Data moves between devices by JAX's collectives and lax.ppermute only.
A program may use at most 128 MiB of HBM per device.

v0:
```python
import math
import jax
import jax.numpy as jnp
from jax import lax
from jax.sharding import PartitionSpec as P

QH = 64
KVH = 8
HD = 128
WINDOW = 1024


def shifted(value, axis, by):
    peers = lax.axis_size(axis)
    pairs = [(i, i + by) for i in range(peers) if 0 <= i + by < peers]
    return lax.ppermute(value, axis, pairs)


def head_grads(query_block, grad_block, keys_head, values_head, allowed, score_scale):
    scores = (
        jnp.einsum("rgd,ed->gre", query_block, keys_head, preferred_element_type=jnp.float32)
        * score_scale
    )
    masked = jnp.where(allowed[None], scores, -jnp.inf)
    highest = jnp.max(masked, axis=-1, keepdims=True)
    weights = jnp.exp(masked - highest)
    probs = weights / jnp.sum(weights, axis=-1, keepdims=True)
    probs_b = probs.astype(jnp.bfloat16)
    attn_out = jnp.einsum("gre,ed->rgd", probs_b, values_head, preferred_element_type=jnp.float32)
    delta = jnp.sum(grad_block.astype(jnp.float32) * attn_out, axis=-1)
    dprobs = jnp.einsum("rgd,ed->gre", grad_block, values_head, preferred_element_type=jnp.float32)
    dscores = probs * (dprobs - jnp.transpose(delta)[:, :, None])
    dscores_b = dscores.astype(jnp.bfloat16)
    grad_query = (
        jnp.einsum("gre,ed->rgd", dscores_b, keys_head, preferred_element_type=jnp.float32)
        * score_scale
    )
    grad_key = (
        jnp.einsum("gre,rgd->ed", dscores_b, query_block, preferred_element_type=jnp.float32)
        * score_scale
    )
    grad_value = jnp.einsum("gre,rgd->ed", probs_b, grad_block, preferred_element_type=jnp.float32)
    return (grad_query, grad_key, grad_value)


def body(queries, upstream, shared_kv):
    local_kv = lax.all_to_all(shared_kv, "tp", split_axis=2, concat_axis=1, tiled=True)
    tok_rows = local_kv.shape[1]
    kv_cols = local_kv.shape[2]
    head_size = HD
    local_kv_heads = kv_cols // head_size
    group_size = QH // KVH
    block_heads = max(1, group_size // 2)
    span_blocks = WINDOW // tok_rows
    score_scale = 1.0 / math.sqrt(head_size)
    earlier = [shifted(local_kv, "seq", span_blocks - offset) for offset in range(span_blocks)]
    extended = jnp.concatenate(earlier + [local_kv], axis=1)
    ext_rows = extended.shape[1]
    position = lax.axis_index("seq")
    row_ids = lax.broadcasted_iota(jnp.int32, (tok_rows, ext_rows), 0)
    key_ids = lax.broadcasted_iota(jnp.int32, (tok_rows, ext_rows), 1)
    allowed = (
        (key_ids >= row_ids + 1)
        & (key_ids <= row_ids + WINDOW)
        & (position * tok_rows - WINDOW + key_ids >= 0)
    )
    query_heads = queries.reshape(tok_rows, -1, head_size)
    grad_heads = upstream.reshape(tok_rows, -1, head_size)
    query_parts = []
    key_parts = []
    value_parts = []
    for kv_head in range(local_kv_heads):
        keys_head = extended[0, :, kv_head * head_size : (kv_head + 1) * head_size]
        values_head = extended[1, :, kv_head * head_size : (kv_head + 1) * head_size]
        key_total = jnp.zeros((ext_rows, head_size), jnp.float32)
        value_total = jnp.zeros((ext_rows, head_size), jnp.float32)
        for first_head in range(kv_head * group_size, (kv_head + 1) * group_size, block_heads):
            query_block = query_heads[:, first_head : first_head + block_heads]
            grad_block = grad_heads[:, first_head : first_head + block_heads]
            grad_query, grad_key, grad_value = head_grads(
                query_block, grad_block, keys_head, values_head, allowed, score_scale
            )
            query_parts.append(grad_query)
            key_total = key_total + grad_key
            value_total = value_total + grad_value
        key_parts.append(key_total)
        value_parts.append(value_total)
    d_queries = jnp.concatenate(query_parts, axis=1).reshape(1, tok_rows, -1).astype(jnp.bfloat16)
    grad_ext = jnp.stack([jnp.concatenate(key_parts, axis=1), jnp.concatenate(value_parts, axis=1)])
    own_rows = grad_ext[:, span_blocks * tok_rows :, :]
    for offset in range(span_blocks):
        own_rows = own_rows + shifted(
            grad_ext[:, offset * tok_rows : (offset + 1) * tok_rows, :].astype(jnp.bfloat16),
            "seq",
            offset - span_blocks,
        ).astype(jnp.float32)
    summed = lax.psum(own_rows, "section")
    d_shared_kv = lax.all_to_all(summed, "tp", split_axis=1, concat_axis=2, tiled=True)
    return (d_queries, d_shared_kv)


def solution(mesh):
    in_specs = (P("section", "seq", "tp"), P("section", "seq", "tp"), P(None, ("seq", "tp"), None))
    out_specs = (P("section", "seq", "tp"), P(None, ("seq", "tp"), None))
    return jax.shard_map(body, mesh=mesh, in_specs=in_specs, out_specs=out_specs, check_vma=False)
```

profile of v0, /device:TPU:1, one launch (start us, length us, event | category | flops | bytes accessed | tf_op | source)
XLA Modules:
  0.0 228.5 jit_solution(4104117547018688944)
XLA Ops:
  7.2 1.4 copy.143
  9.6 6.6 %all-to-all-start = ((bf16[4,2,16384]{2,1,0:T(2,128)(2,1)}), bf16[4,2,16384]{2,1,0:T(2,128)(2,1)S(1)}, u32[]{:S(2)}, u32[]{:S(2)}) async-start(bf16[4,2,16384]{2,1,0:T(2,128)(2,1)} %reshape.105), calls=%async_computation | async-start | bytes 524288 | tf_op jit(solution)/shard_map/all_to_all | solution.py:47
  16.2 5.0 %all-to-all-done = bf16[4,2,16384]{2,1,0:T(2,128)(2,1)S(1)} async-done(((bf16[4,2,16384]{2,1,0:T(2,128)(2,1)}), bf16[4,2,16384]{2,1,0:T(2,128)(2,1)S(1)}, u32[]{:S(2)}, u32[]{:S(2)}) %all-to-all-start) | async-done | bytes 262176 | tf_op jit(solution)/shard_map/all_to_all | solution.py:47
  22.6 3.9 %collective-permute-start = (bf16[2,256,256]{2,1,0:T(8,128)(2,1)}, bf16[2,256,256]{2,1,0:T(8,128)(2,1)}, u32[]{:S(2)}, u32[]{:S(2)}) collective-permute-start(bf16[2,256,256]{2,1,0:T(8,128)(2,1)} %bitcast.2), channel_id=1, source_target_pairs={{0,16},{4,20},{8,24},{12,28},{16,32},{20,36},{24,40},{28,44},{32,4... | collective-permute-start | bytes 786440 | tf_op jit(solution)/shard_map/ppermute | solution.py:16
  28.2 4.3 %collective-permute-start.2 = (bf16[2,256,256]{2,1,0:T(8,128)(2,1)}, bf16[2,256,256]{2,1,0:T(8,128)(2,1)}, u32[]{:S(2)}, u32[]{:S(2)}) collective-permute-start(bf16[2,256,256]{2,1,0:T(8,128)(2,1)} %bitcast.2), channel_id=1, source_target_pairs={{0,8},{4,12},{8,16},{12,20},{16,24},{20,28},{24,32},{28,36},{32,40... | collective-permute-start | bytes 786440 | tf_op jit(solution)/shard_map/ppermute | solution.py:16
  32.4 6.7 %collective-permute-start.1 = (bf16[2,256,256]{2,1,0:T(8,128)(2,1)}, bf16[2,256,256]{2,1,0:T(8,128)(2,1)}, u32[]{:S(2)}, u32[]{:S(2)}) collective-permute-start(bf16[2,256,256]{2,1,0:T(8,128)(2,1)} %bitcast.2), channel_id=1, source_target_pairs={{0,12},{4,16},{8,20},{12,24},{16,28},{20,32},{24,36},{28,40},{32,4... | collective-permute-start | bytes 786440 | tf_op jit(solution)/shard_map/ppermute | solution.py:16
  39.2 1.5 copy.145
  44.3 2.6 %collective-permute-start.3 = (bf16[2,256,256]{2,1,0:T(8,128)(2,1)}, bf16[2,256,256]{2,1,0:T(8,128)(2,1)S(1)}, u32[]{:S(2)}, u32[]{:S(2)}) collective-permute-start(bf16[2,256,256]{2,1,0:T(8,128)(2,1)} %bitcast.2), channel_id=1, source_target_pairs={{0,4},{4,8},{8,12},{12,16},{16,20},{20,24},{24,28},{28,32},{32,36}... | collective-permute-start | bytes 786440 | tf_op jit(solution)/shard_map/ppermute | solution.py:16
  51.9 5.3 %exponential_reduce_fusion.3 = (f32[4,256]{1,0:T(4,128)S(1)}, f32[4,256,1280]{1,2,0:T(8,128)}) fusion(pred[256,1280]{0,1:T(8,128)(4,1)} %fusion.28, bf16[256,16,128]{0,2,1:T(8,128)(2,1)S(1)} %bitcast.227, bf16[2,1280,256]{2,1,0:T(8,128)(2,1)S(1)} %constant_dynamic-update-slice_fusion), kind=kOutput, calls=%fused_computation.31 | convolution fusion | flops 340788480 | bytes 6164480 | tf_op jit(solution)/shard_map/sub | solution.py:26
  57.1 5.1 %exponential_reduce_fusion.1 = (f32[4,256]{1,0:T(4,128)S(1)}, f32[4,256,1280]{1,2,0:T(8,128)}) fusion(pred[256,1280]{0,1:T(8,128)(4,1)} %fusion.28, bf16[256,16,128]{0,2,1:T(8,128)(2,1)S(1)} %bitcast.228, bf16[2,1280,256]{2,1,0:T(8,128)(2,1)S(1)} %constant_dynamic-update-slice_fusion), kind=kOutput, calls=%fused_computation.27 | convolution fusion | flops 340788480 | bytes 6164480 | tf_op jit(solution)/shard_map/sub | solution.py:26
  62.3 5.1 %exponential_reduce_fusion.2 = (f32[4,256]{1,0:T(4,128)S(1)}, f32[4,256,1280]{1,2,0:T(8,128)}) fusion(pred[256,1280]{0,1:T(8,128)(4,1)} %fusion.28, bf16[256,16,128]{0,2,1:T(8,128)(2,1)S(1)} %bitcast.229, bf16[2,1280,256]{2,1,0:T(8,128)(2,1)S(1)} %constant_dynamic-update-slice_fusion), kind=kOutput, calls=%fused_computation.29 | convolution fusion | flops 340788480 | bytes 6164480 | tf_op jit(solution)/shard_map/sub | solution.py:26
  67.4 5.1 %exponential_reduce_fusion = (f32[4,256]{1,0:T(4,128)S(1)}, f32[4,256,1280]{1,2,0:T(8,128)}) fusion(pred[256,1280]{0,1:T(8,128)(4,1)} %fusion.28, bf16[256,16,128]{0,2,1:T(8,128)(2,1)S(1)} %bitcast.230, bf16[2,1280,256]{2,1,0:T(8,128)(2,1)S(1)} %constant_dynamic-update-slice_fusion), kind=kOutput, calls=%fused_computation.25 | convolution fusion | flops 340788480 | bytes 6164480 | tf_op jit(solution)/shard_map/sub | solution.py:26
  72.5 4.0 %fusion.23 = bf16[4,256,1280]{1,2,0:T(8,128)(2,1)S(1)} fusion(f32[4,256]{1,0:T(4,128)S(1)} %get-tuple-element.24, f32[4,256,1280]{1,2,0:T(8,128)} %get-tuple-element.25), kind=kLoop, calls=%fused_computation.50 | loop fusion | flops 2621440 | bytes 7868416 | tf_op jit(solution)/shard_map/convert_element_type | solution.py:28
  81.2 1.6 fusion.25
  88.6 1.4 fusion.24
  90.0 1.3 fusion.38
  95.7 1.4 fusion.26
  99.8 2.5 %fusion.9 = bf16[4,256,1280]{1,2,0:T(8,128)(2,1)S(1)} fusion(f32[4,256]{1,0:T(4,128)S(1)} %bitcast.240, f32[4,256]{1,0:T(4,128)S(1)} %get-tuple-element.18, f32[4,256,1280]{1,2,0:T(8,128)S(1)} %bitcast.220, bf16[2,1280,256]{2,1,0:T(8,128)(2,1)S(1)} %copy-done.5, bf16[256,16,128]{0,2,1:T(8,128)(2,1)} %bitcast.218), kind=kOutput, calls=%fused_computation.10 | convolution fusion | flops 340787200 | bytes 8462336 | tf_op jit(solution)/shard_map/rgd,ed->gre/dot_general | solution.py:31
  104.7 1.3 collective-permute-start.4
  106.0 1.3 collective-permute-start.7
  107.3 1.3 collective-permute-start.6
  108.6 1.3 collective-permute-start.5
  110.5 22.5 %collective-permute-done.4 = bf16[2,256,256]{1,2,0:T(8,128)(2,1)S(1)} collective-permute-done((bf16[2,256,256]{1,2,0:T(8,128)(2,1)S(1)}, bf16[2,256,256]{1,2,0:T(8,128)(2,1)S(1)}, u32[]{:S(2)}, u32[]{:S(2)}) %collective-permute-start.4) | collective-permute-done | bytes 262176 | tf_op jit(solution)/shard_map/ppermute | solution.py:16
  133.0 6.1 %collective-permute-done.5 = bf16[2,256,256]{1,2,0:T(8,128)(2,1)S(1)} collective-permute-done((bf16[2,256,256]{1,2,0:T(8,128)(2,1)S(1)}, bf16[2,256,256]{1,2,0:T(8,128)(2,1)S(1)}, u32[]{:S(2)}, u32[]{:S(2)}) %collective-permute-start.5) | collective-permute-done | bytes 262176 | tf_op jit(solution)/shard_map/ppermute | solution.py:16
  140.1 3.2 %fusion.42 = bf16[256,4,128]{0,2,1:T(8,128)(2,1)} fusion(bf16[4,256,1280]{1,2,0:T(8,128)(2,1)} %copy-done.2, bf16[2,1280,256]{2,1,0:T(8,128)(2,1)} %copy-done.4), kind=kOutput, calls=%fused_computation.81 | convolution fusion | flops 335806464 | bytes 3211264 | tf_op jit(solution)/shard_map/gre,ed->rgd/dot_general | solution.py:35
  143.3 2.2 fusion.43
  145.5 59.1 %all-reduce.2.cloned.1.call-done = f32[2,256,256]{1,2,0:T(8,128)} async-done(((f32[2,256,256]{1,2,0:T(8,128)}), f32[2,256,256]{1,2,0:T(8,128)}) %all-reduce.2.cloned.1.call-update) | async-done | bytes 524304 | tf_op jit(solution)/shard_map/psum | solution.py:97
  204.6 2.0 copy.191
  206.6 6.3 %all-to-all-start.1 = ((f32[2,256,256]{2,0,1:T(2,128)}), f32[2,256,256]{2,0,1:T(2,128)S(1)}, u32[]{:S(2)}, u32[]{:S(2)}) async-start(f32[2,256,256]{2,0,1:T(2,128)} %copy.191), calls=%async_computation.1 | async-start | bytes 1048576 | tf_op jit(solution)/shard_map/all_to_all | solution.py:98
  213.0 1.6 fusion.41
  214.7 1.4 copy.194
  216.1 4.7 %all-to-all-done.1 = f32[2,256,256]{2,0,1:T(2,128)S(1)} async-done(((f32[2,256,256]{2,0,1:T(2,128)}), f32[2,256,256]{2,0,1:T(2,128)S(1)}, u32[]{:S(2)}, u32[]{:S(2)}) %all-to-all-start.1) | async-done | bytes 524320 | tf_op jit(solution)/shard_map/all_to_all | solution.py:98
  (98 shorter events, 35.0 us)
Async XLA Ops:
  7.2 20.5 %copy-start.12 = (bf16[1,256,2048]{2,1,0:T(8,128)(2,1)S(1)}, bf16[1,256,2048]{2,1,0:T(8,128)(2,1)}, u32[]{:S(2)}) copy-start(bf16[1,256,2048]{2,1,0:T(8,128)(2,1)} %param.4) | copy-start | bytes 3145732
  9.6 11.6 %all-to-all-start = ((bf16[4,2,16384]{2,1,0:T(2,128)(2,1)}), bf16[4,2,16384]{2,1,0:T(2,128)(2,1)S(1)}, u32[]{:S(2)}, u32[]{:S(2)}) async-start(bf16[4,2,16384]{2,1,0:T(2,128)(2,1)} %reshape.105), calls=%async_computation | async-start | bytes 524288 | tf_op jit(solution)/shard_map/all_to_all | solution.py:47
  16.2 188.4 %all-reduce.2.cloned.1.call-start = ((), (), s32[]{:S(2)}) async-start(), calls=%async_computation.2 | async-start | bytes 1048576 | tf_op jit(solution)/shard_map/psum | solution.py:97
  22.6 24.3 %collective-permute-start = (bf16[2,256,256]{2,1,0:T(8,128)(2,1)}, bf16[2,256,256]{2,1,0:T(8,128)(2,1)}, u32[]{:S(2)}, u32[]{:S(2)}) collective-permute-start(bf16[2,256,256]{2,1,0:T(8,128)(2,1)} %bitcast.2), channel_id=1, source_target_pairs={{0,16},{4,20},{8,24},{12,28},{16,32},{20,36},{24,40},{28,44},{32,4... | collective-permute-start | bytes 786440 | tf_op jit(solution)/shard_map/ppermute | solution.py:16
  28.2 70.3 %copy-start.3 = (bf16[1,256,2048]{1,2,0:T(8,128)(2,1)}, bf16[1,256,2048]{1,2,0:T(8,128)(2,1)S(1)}, u32[]{:S(2)}) copy-start(bf16[1,256,2048]{1,2,0:T(8,128)(2,1)S(1)} %copy.147) | copy-start | bytes 3145732
  28.2 20.7 %collective-permute-start.2 = (bf16[2,256,256]{2,1,0:T(8,128)(2,1)}, bf16[2,256,256]{2,1,0:T(8,128)(2,1)}, u32[]{:S(2)}, u32[]{:S(2)}) collective-permute-start(bf16[2,256,256]{2,1,0:T(8,128)(2,1)} %bitcast.2), channel_id=1, source_target_pairs={{0,8},{4,12},{8,16},{12,20},{16,24},{20,28},{24,32},{28,36},{32,40... | collective-permute-start | bytes 786440 | tf_op jit(solution)/shard_map/ppermute | solution.py:16
  32.4 15.5 %collective-permute-start.1 = (bf16[2,256,256]{2,1,0:T(8,128)(2,1)}, bf16[2,256,256]{2,1,0:T(8,128)(2,1)}, u32[]{:S(2)}, u32[]{:S(2)}) collective-permute-start(bf16[2,256,256]{2,1,0:T(8,128)(2,1)} %bitcast.2), channel_id=1, source_target_pairs={{0,12},{4,16},{8,20},{12,24},{16,28},{20,32},{24,36},{28,40},{32,4... | collective-permute-start | bytes 786440 | tf_op jit(solution)/shard_map/ppermute | solution.py:16
  40.7 45.6 %copy-start.6 = (bf16[1,256,2048]{1,2,0:T(8,128)(2,1)}, bf16[1,256,2048]{1,2,0:T(8,128)(2,1)S(1)}, u32[]{:S(2)}) copy-start(bf16[1,256,2048]{1,2,0:T(8,128)(2,1)S(1)} %copy.145) | copy-start | bytes 3145732
  44.3 6.6 %collective-permute-start.3 = (bf16[2,256,256]{2,1,0:T(8,128)(2,1)}, bf16[2,256,256]{2,1,0:T(8,128)(2,1)S(1)}, u32[]{:S(2)}, u32[]{:S(2)}) collective-permute-start(bf16[2,256,256]{2,1,0:T(8,128)(2,1)} %bitcast.2), channel_id=1, source_target_pairs={{0,4},{4,8},{8,12},{12,16},{16,20},{20,24},{24,28},{28,32},{32,36}... | collective-permute-start | bytes 786440 | tf_op jit(solution)/shard_map/ppermute | solution.py:16
  51.9 45.3 %copy-start.4 = (bf16[2,1280,256]{2,1,0:T(8,128)(2,1)}, bf16[2,1280,256]{2,1,0:T(8,128)(2,1)S(1)}, u32[]{:S(2)}) copy-start(bf16[2,1280,256]{2,1,0:T(8,128)(2,1)S(1)} %constant_dynamic-update-slice_fusion) | copy-start | bytes 3932164
  72.5 6.3 %slice-start.6 = ((s8[5242880]{0:T(1024)(128)(4,1)}), s8[4194304]{0:T(1024)(128)(4,1)S(1)}, s32[]{:S(2)}) async-start(s8[5242880]{0:T(1024)(128)(4,1)} %bitcast.225), calls=%async_computation.9 | async-start | bytes 8388608
  76.5 2.3 %slice-start.7 = ((s8[5242880]{0:T(1024)(128)(4,1)}), s8[1048576]{0:T(1024)(128)(4,1)S(1)}, s32[]{:S(2)}) async-start(s8[5242880]{0:T(1024)(128)(4,1)} %bitcast.225), calls=%async_computation.10 | async-start | bytes 2097152
  78.8 2.2 slice-start.4
  78.8 2.5 %slice-start.5 = ((s8[5242880]{0:T(1024)(128)(4,1)}), s8[1048576]{0:T(1024)(128)(4,1)S(1)}, s32[]{:S(2)}) async-start(s8[5242880]{0:T(1024)(128)(4,1)} %bitcast.223), calls=%async_computation.8 | async-start | bytes 2097152
  85.2 2.7 %slice-start.2 = ((s8[5242880]{0:T(1024)(128)(4,1)}), s8[4194304]{0:T(1024)(128)(4,1)S(1)}, s32[]{:S(2)}) async-start(s8[5242880]{0:T(1024)(128)(4,1)} %bitcast.221), calls=%async_computation.5 | async-start | bytes 8388608
  85.2 3.4 %slice-start.3 = ((s8[5242880]{0:T(1024)(128)(4,1)}), s8[1048576]{0:T(1024)(128)(4,1)S(1)}, s32[]{:S(2)}) async-start(s8[5242880]{0:T(1024)(128)(4,1)} %bitcast.221), calls=%async_computation.6 | async-start | bytes 2097152
  86.3 1.6 copy-start.2
  88.6 1.4 copy-start.9
  92.3 2.4 %slice-start = ((s8[5242880]{0:T(1024)(128)(4,1)}), s8[4194304]{0:T(1024)(128)(4,1)S(1)}, s32[]{:S(2)}) async-start(s8[5242880]{0:T(1024)(128)(4,1)} %bitcast.219), calls=%async_computation.3 | async-start | bytes 8388608
  92.3 3.4 %slice-start.1 = ((s8[5242880]{0:T(1024)(128)(4,1)}), s8[1048576]{0:T(1024)(128)(4,1)S(1)}, s32[]{:S(2)}) async-start(s8[5242880]{0:T(1024)(128)(4,1)} %bitcast.219), calls=%async_computation.4 | async-start | bytes 2097152
  93.5 8.8 %copy-start = (bf16[4,256,1280]{1,2,0:T(8,128)(2,1)}, bf16[4,256,1280]{1,2,0:T(8,128)(2,1)S(1)}, u32[]{:S(2)}) copy-start(bf16[4,256,1280]{1,2,0:T(8,128)(2,1)S(1)} %fusion.13) | copy-start | bytes 7864324
  95.7 1.4 copy-start.8
  98.5 1.3 copy-start.5
  99.8 2.5 %copy-start.7 = (bf16[1,256,2048]{1,2,0:T(8,128)(2,1)S(1)}, bf16[1,256,2048]{1,2,0:T(8,128)(2,1)}, u32[]{:S(2)}) copy-start(bf16[1,256,2048]{1,2,0:T(8,128)(2,1)} %copy-done.6) | copy-start | bytes 3145732
  104.7 28.2 %collective-permute-start.4 = (bf16[2,256,256]{1,2,0:T(8,128)(2,1)S(1)}, bf16[2,256,256]{1,2,0:T(8,128)(2,1)S(1)}, u32[]{:S(2)}, u32[]{:S(2)}) collective-permute-start(bf16[2,256,256]{1,2,0:T(8,128)(2,1)S(1)} %get-tuple-element.10), channel_id=1, source_target_pairs={{16,0},{20,4},{24,8},{28,12},{32,16},{36,20},{40,24},{44,28},{48,3... | collective-permute-start | bytes 786440 | tf_op jit(solution)/shard_map/ppermute | solution.py:16
  106.0 26.9 %collective-permute-start.7 = (bf16[2,256,256]{1,2,0:T(8,128)(2,1)S(1)}, bf16[2,256,256]{1,2,0:T(8,128)(2,1)S(1)}, u32[]{:S(2)}, u32[]{:S(2)}) collective-permute-start(bf16[2,256,256]{1,2,0:T(8,128)(2,1)S(1)} %get-tuple-element.11), channel_id=1, source_target_pairs={{4,0},{8,4},{12,8},{16,12},{20,16},{24,20},{28,24},{32,28},{36,32}... | collective-permute-start | bytes 786440 | tf_op jit(solution)/shard_map/ppermute | solution.py:16
  107.3 25.6 %collective-permute-start.6 = (bf16[2,256,256]{1,2,0:T(8,128)(2,1)S(1)}, bf16[2,256,256]{1,2,0:T(8,128)(2,1)S(1)}, u32[]{:S(2)}, u32[]{:S(2)}) collective-permute-start(bf16[2,256,256]{1,2,0:T(8,128)(2,1)S(1)} %get-tuple-element.12), channel_id=1, source_target_pairs={{8,0},{12,4},{16,8},{20,12},{24,16},{28,20},{32,24},{36,28},{40,32... | collective-permute-start | bytes 786440 | tf_op jit(solution)/shard_map/ppermute | solution.py:16
  108.6 30.4 %collective-permute-start.5 = (bf16[2,256,256]{1,2,0:T(8,128)(2,1)S(1)}, bf16[2,256,256]{1,2,0:T(8,128)(2,1)S(1)}, u32[]{:S(2)}, u32[]{:S(2)}) collective-permute-start(bf16[2,256,256]{1,2,0:T(8,128)(2,1)S(1)} %get-tuple-element.13), channel_id=1, source_target_pairs={{12,0},{16,4},{20,8},{24,12},{28,16},{32,20},{36,24},{40,28},{44,3... | collective-permute-start | bytes 786440 | tf_op jit(solution)/shard_map/ppermute | solution.py:16
  140.1 3.3 %copy-start.1 = (bf16[4,256,1280]{1,2,0:T(8,128)(2,1)S(1)}, bf16[4,256,1280]{1,2,0:T(8,128)(2,1)}, u32[]{:S(2)}) copy-start(bf16[4,256,1280]{1,2,0:T(8,128)(2,1)} %copy-done) | copy-start | bytes 7864324
  206.6 14.2 %all-to-all-start.1 = ((f32[2,256,256]{2,0,1:T(2,128)}), f32[2,256,256]{2,0,1:T(2,128)S(1)}, u32[]{:S(2)}, u32[]{:S(2)}) async-start(f32[2,256,256]{2,0,1:T(2,128)} %copy.191), calls=%async_computation.1 | async-start | bytes 1048576 | tf_op jit(solution)/shard_map/all_to_all | solution.py:98
  213.0 1.6 copy-start.13
  213.0 1.6 copy-start.14
  (2 other events, 2.0 us)
Sparse Core Ops, SparseCore 0:
  140.2 64.3 all-reduce.1
where the time goes:
time: 229 us
  waiting for transfers between devices  98.4 us (43%)
  matrix products  47 us (21%)
  starting transfers between devices  35.5 us (16%)
  local copies, waits for them, and re-layouts  22.1 us (10%)
  between operations  14.6 us (6%)
  other arithmetic  11 us (5%)
    psum x1, waiting for transfers between devices, body(): summed = lax.psum(own_rows, 'section')  59.1 us
    ppermute x8, waiting for transfers between devices, shifted(): return lax.ppermute(value, axis, pairs)  29.6 us
    ppermute x8, starting transfers between devices, shifted(): return lax.ppermute(value, axis, pairs)  22.6 us
    sub x4, matrix products, head_grads(): weights = jnp.exp(masked - highest)  20.6 us
    unnamed x61, local copies, waits for them, and re-layouts  17.1 us
    convert_element_type x4, other arithmetic, head_grads(): probs_b = probs.astype(jnp.bfloat16)  8.43 us
    dot_general x4, matrix products, head_grads(): jnp.einsum('gre,ed->rgd', dscores_b, keys_head, preferred_element_type=jn...  7.58 us
    all_to_all x1, starting transfers between devices, body(): lax.all_to_all(shared_kv, 'tp', split_axis=2, concat_axis=1, tiled=True)  6.57 us
  transfers between devices with their start and end apart: 11, of which 6 were waited for; matrix products, arithmetic and copies ran while one was open for 8% of the time, Pallas kernels for 0%

commit v1 on v0

--- a/solution.py
+++ b/solution.py
@@ -94,7 +94,9 @@
             "seq",
             offset - span_blocks,
         ).astype(jnp.float32)
-    summed = lax.psum(own_rows, "section")
+    summed = own_rows
+    for hop in (1, 2):
+        summed = summed + lax.ppermute(summed, "section", [(dev, dev ^ hop) for dev in range(4)])
     d_shared_kv = lax.all_to_all(summed, "tp", split_axis=1, concat_axis=2, tiled=True)
     return (d_queries, d_shared_kv)
 

time: 229 us -> 191 us (0.83)
  the two profiles are of different devices: /device:TPU:1 before, /device:TPU:80 now
where the time goes in v1:
time: 191 us; the launch traced here: 190 us
  waiting for transfers between devices  76.4 us (40%)
  matrix products  44 us (23%)
  starting transfers between devices  38.8 us (20%)
  local copies, waits for them, and re-layouts  19.1 us (10%)
  other arithmetic  10.4 us (5%)
    ppermute x8, waiting for transfers between devices, shifted(): return lax.ppermute(value, axis, pairs)  45.4 us
    ppermute x8, starting transfers between devices, shifted(): return lax.ppermute(value, axis, pairs)  27.3 us
    sub x4, matrix products, head_grads(): weights = jnp.exp(masked - highest)  20.6 us
    ppermute x2, waiting for transfers between devices, body(): lax.ppermute(summed, 'section', [(dev, dev ^ hop) for dev in range(4)])  19.4 us
    unnamed x55, local copies, waits for them, and re-layouts  15.1 us
    convert_element_type x4, other arithmetic, head_grads(): probs_b = probs.astype(jnp.bfloat16)  8.43 us
    all_to_all x1, waiting for transfers between devices, body(): lax.all_to_all(shared_kv, 'tp', split_axis=2, concat_axis=1, tiled=True)  5.94 us
    dot_general x4, matrix products, head_grads(): jnp.einsum('rgd,ed->gre', grad_block, values_head, preferred_element_type...  5.86 us
  transfers between devices with their start and end apart: 12, of which 9 were waited for; matrix products, arithmetic and copies ran while one was open for 8% of the time, Pallas kernels for 0%

profile of v1, /device:TPU:80, one launch (start us, length us, event | category | flops | bytes accessed | tf_op | source)
XLA Modules:
  0.0 189.9 jit_solution(5957801366178075595)
XLA Ops:
  3.1 3.4 %all-to-all-start = ((bf16[4,2,16384]{2,1,0:T(2,128)(2,1)}), bf16[4,2,16384]{2,1,0:T(2,128)(2,1)S(1)}, u32[]{:S(2)}, u32[]{:S(2)}) async-start(bf16[4,2,16384]{2,1,0:T(2,128)(2,1)} %reshape.105), calls=%async_computation | async-start | bytes 524288 | tf_op jit(solution)/shard_map/all_to_all | solution.py:47
  6.5 5.9 %all-to-all-done = bf16[4,2,16384]{2,1,0:T(2,128)(2,1)S(1)} async-done(((bf16[4,2,16384]{2,1,0:T(2,128)(2,1)}), bf16[4,2,16384]{2,1,0:T(2,128)(2,1)S(1)}, u32[]{:S(2)}, u32[]{:S(2)}) %all-to-all-start) | async-done | bytes 262176 | tf_op jit(solution)/shard_map/all_to_all | solution.py:47
  13.9 6.4 %collective-permute-start = (bf16[2,256,256]{2,1,0:T(8,128)(2,1)}, bf16[2,256,256]{2,1,0:T(8,128)(2,1)}, u32[]{:S(2)}, u32[]{:S(2)}) collective-permute-start(bf16[2,256,256]{2,1,0:T(8,128)(2,1)} %bitcast.2), channel_id=1, source_target_pairs={{0,16},{4,20},{8,24},{12,28},{16,32},{20,36},{24,40},{28,44},{32,4... | collective-permute-start | bytes 786440 | tf_op jit(solution)/shard_map/ppermute | solution.py:16
  21.9 2.9 %collective-permute-start.2 = (bf16[2,256,256]{2,1,0:T(8,128)(2,1)}, bf16[2,256,256]{2,1,0:T(8,128)(2,1)}, u32[]{:S(2)}, u32[]{:S(2)}) collective-permute-start(bf16[2,256,256]{2,1,0:T(8,128)(2,1)} %bitcast.2), channel_id=1, source_target_pairs={{0,8},{4,12},{8,16},{12,20},{16,24},{20,28},{24,32},{28,36},{32,40... | collective-permute-start | bytes 786440 | tf_op jit(solution)/shard_map/ppermute | solution.py:16
  24.8 3.2 %collective-permute-start.1 = (bf16[2,256,256]{2,1,0:T(8,128)(2,1)}, bf16[2,256,256]{2,1,0:T(8,128)(2,1)}, u32[]{:S(2)}, u32[]{:S(2)}) collective-permute-start(bf16[2,256,256]{2,1,0:T(8,128)(2,1)} %bitcast.2), channel_id=1, source_target_pairs={{0,12},{4,16},{8,20},{12,24},{16,28},{20,32},{24,36},{28,40},{32,4... | collective-permute-start | bytes 786440 | tf_op jit(solution)/shard_map/ppermute | solution.py:16
  28.1 1.5 copy.145
  33.1 5.3 %collective-permute-start.3 = (bf16[2,256,256]{2,1,0:T(8,128)(2,1)}, bf16[2,256,256]{2,1,0:T(8,128)(2,1)S(1)}, u32[]{:S(2)}, u32[]{:S(2)}) collective-permute-start(bf16[2,256,256]{2,1,0:T(8,128)(2,1)} %bitcast.2), channel_id=1, source_target_pairs={{0,4},{4,8},{8,12},{12,16},{16,20},{20,24},{24,28},{28,32},{32,36}... | collective-permute-start | bytes 786440 | tf_op jit(solution)/shard_map/ppermute | solution.py:16
  39.4 10.3 %collective-permute-done.1 = bf16[2,256,256]{2,1,0:T(8,128)(2,1)} collective-permute-done((bf16[2,256,256]{2,1,0:T(8,128)(2,1)}, bf16[2,256,256]{2,1,0:T(8,128)(2,1)}, u32[]{:S(2)}, u32[]{:S(2)}) %collective-permute-start.1) | collective-permute-done | bytes 262176 | tf_op jit(solution)/shard_map/ppermute | solution.py:16
  51.6 2.3 %collective-permute-done.3 = bf16[2,256,256]{2,1,0:T(8,128)(2,1)S(1)} collective-permute-done((bf16[2,256,256]{2,1,0:T(8,128)(2,1)}, bf16[2,256,256]{2,1,0:T(8,128)(2,1)S(1)}, u32[]{:S(2)}, u32[]{:S(2)}) %collective-permute-start.3) | collective-permute-done | bytes 262176 | tf_op jit(solution)/shard_map/ppermute | solution.py:16
  54.9 5.3 %exponential_reduce_fusion.3 = (f32[4,256]{1,0:T(4,128)S(1)}, f32[4,256,1280]{1,2,0:T(8,128)}) fusion(pred[256,1280]{0,1:T(8,128)(4,1)} %fusion.28, bf16[256,16,128]{0,2,1:T(8,128)(2,1)S(1)} %bitcast.227, bf16[2,1280,256]{2,1,0:T(8,128)(2,1)S(1)} %constant_dynamic-update-slice_fusion), kind=kOutput, calls=%fused_computation.31 | convolution fusion | flops 340788480 | bytes 6164480 | tf_op jit(solution)/shard_map/sub | solution.py:26
  60.2 5.1 %exponential_reduce_fusion.1 = (f32[4,256]{1,0:T(4,128)S(1)}, f32[4,256,1280]{1,2,0:T(8,128)}) fusion(pred[256,1280]{0,1:T(8,128)(4,1)} %fusion.28, bf16[256,16,128]{0,2,1:T(8,128)(2,1)S(1)} %bitcast.228, bf16[2,1280,256]{2,1,0:T(8,128)(2,1)S(1)} %constant_dynamic-update-slice_fusion), kind=kOutput, calls=%fused_computation.27 | convolution fusion | flops 340788480 | bytes 6164480 | tf_op jit(solution)/shard_map/sub | solution.py:26
  65.3 5.1 %exponential_reduce_fusion.2 = (f32[4,256]{1,0:T(4,128)S(1)}, f32[4,256,1280]{1,2,0:T(8,128)}) fusion(pred[256,1280]{0,1:T(8,128)(4,1)} %fusion.28, bf16[256,16,128]{0,2,1:T(8,128)(2,1)S(1)} %bitcast.229, bf16[2,1280,256]{2,1,0:T(8,128)(2,1)S(1)} %constant_dynamic-update-slice_fusion), kind=kOutput, calls=%fused_computation.29 | convolution fusion | flops 340788480 | bytes 6164480 | tf_op jit(solution)/shard_map/sub | solution.py:26
  70.4 5.1 %exponential_reduce_fusion = (f32[4,256]{1,0:T(4,128)S(1)}, f32[4,256,1280]{1,2,0:T(8,128)}) fusion(pred[256,1280]{0,1:T(8,128)(4,1)} %fusion.28, bf16[256,16,128]{0,2,1:T(8,128)(2,1)S(1)} %bitcast.230, bf16[2,1280,256]{2,1,0:T(8,128)(2,1)S(1)} %constant_dynamic-update-slice_fusion), kind=kOutput, calls=%fused_computation.25 | convolution fusion | flops 340788480 | bytes 6164480 | tf_op jit(solution)/shard_map/sub | solution.py:26
  75.5 4.0 %fusion.23 = bf16[4,256,1280]{1,2,0:T(8,128)(2,1)S(1)} fusion(f32[4,256]{1,0:T(4,128)S(1)} %get-tuple-element.24, f32[4,256,1280]{1,2,0:T(8,128)} %get-tuple-element.25), kind=kLoop, calls=%fused_computation.50 | loop fusion | flops 2621440 | bytes 7868416 | tf_op jit(solution)/shard_map/convert_element_type | solution.py:28
  84.2 1.6 fusion.25
  90.6 1.4 fusion.24
  100.9 2.5 %fusion.9 = bf16[4,256,1280]{1,2,0:T(8,128)(2,1)S(1)} fusion(f32[4,256]{1,0:T(4,128)S(1)} %bitcast.240, f32[4,256]{1,0:T(4,128)S(1)} %get-tuple-element.18, f32[4,256,1280]{1,2,0:T(8,128)S(1)} %bitcast.220, bf16[2,1280,256]{2,1,0:T(8,128)(2,1)S(1)} %copy-done.2, bf16[256,16,128]{0,2,1:T(8,128)(2,1)} %bitcast.218), kind=kOutput, calls=%fused_computation.10 | convolution fusion | flops 340787200 | bytes 8462336 | tf_op jit(solution)/shard_map/rgd,ed->gre/dot_general | solution.py:31
  105.8 1.9 %collective-permute-start.4 = (bf16[2,256,256]{1,2,0:T(8,128)(2,1)S(1)}, bf16[2,256,256]{1,2,0:T(8,128)(2,1)S(1)}, u32[]{:S(2)}, u32[]{:S(2)}) collective-permute-start(bf16[2,256,256]{1,2,0:T(8,128)(2,1)S(1)} %get-tuple-element.10), channel_id=1, source_target_pairs={{16,0},{20,4},{24,8},{28,12},{32,16},{36,20},{40,24},{44,28},{48,3... | collective-permute-start | bytes 786440 | tf_op jit(solution)/shard_map/ppermute | solution.py:16
  107.8 3.8 %collective-permute-start.7 = (bf16[2,256,256]{1,2,0:T(8,128)(2,1)S(1)}, bf16[2,256,256]{1,2,0:T(8,128)(2,1)S(1)}, u32[]{:S(2)}, u32[]{:S(2)}) collective-permute-start(bf16[2,256,256]{1,2,0:T(8,128)(2,1)S(1)} %get-tuple-element.11), channel_id=1, source_target_pairs={{4,0},{8,4},{12,8},{16,12},{20,16},{24,20},{28,24},{32,28},{36,32}... | collective-permute-start | bytes 786440 | tf_op jit(solution)/shard_map/ppermute | solution.py:16
  111.5 1.9 %collective-permute-start.6 = (bf16[2,256,256]{1,2,0:T(8,128)(2,1)S(1)}, bf16[2,256,256]{1,2,0:T(8,128)(2,1)S(1)}, u32[]{:S(2)}, u32[]{:S(2)}) collective-permute-start(bf16[2,256,256]{1,2,0:T(8,128)(2,1)S(1)} %get-tuple-element.12), channel_id=1, source_target_pairs={{8,0},{12,4},{16,8},{20,12},{24,16},{28,20},{32,24},{36,28},{40,32... | collective-permute-start | bytes 786440 | tf_op jit(solution)/shard_map/ppermute | solution.py:16
  113.5 1.9 %collective-permute-start.5 = (bf16[2,256,256]{1,2,0:T(8,128)(2,1)S(1)}, bf16[2,256,256]{1,2,0:T(8,128)(2,1)S(1)}, u32[]{:S(2)}, u32[]{:S(2)}) collective-permute-start(bf16[2,256,256]{1,2,0:T(8,128)(2,1)S(1)} %get-tuple-element.13), channel_id=1, source_target_pairs={{12,0},{16,4},{20,8},{24,12},{28,16},{32,20},{36,24},{40,28},{44,3... | collective-permute-start | bytes 786440 | tf_op jit(solution)/shard_map/ppermute | solution.py:16
  115.4 8.5 %collective-permute-done.4 = bf16[2,256,256]{1,2,0:T(8,128)(2,1)S(1)} collective-permute-done((bf16[2,256,256]{1,2,0:T(8,128)(2,1)S(1)}, bf16[2,256,256]{1,2,0:T(8,128)(2,1)S(1)}, u32[]{:S(2)}, u32[]{:S(2)}) %collective-permute-start.4) | collective-permute-done | bytes 262176 | tf_op jit(solution)/shard_map/ppermute | solution.py:16
  123.9 7.0 %collective-permute-done.7 = bf16[2,256,256]{1,2,0:T(8,128)(2,1)S(1)} collective-permute-done((bf16[2,256,256]{1,2,0:T(8,128)(2,1)S(1)}, bf16[2,256,256]{1,2,0:T(8,128)(2,1)S(1)}, u32[]{:S(2)}, u32[]{:S(2)}) %collective-permute-start.7) | collective-permute-done | bytes 262176 | tf_op jit(solution)/shard_map/ppermute | solution.py:16
  131.0 17.3 %collective-permute-done.5 = bf16[2,256,256]{1,2,0:T(8,128)(2,1)S(1)} collective-permute-done((bf16[2,256,256]{1,2,0:T(8,128)(2,1)S(1)}, bf16[2,256,256]{1,2,0:T(8,128)(2,1)S(1)}, u32[]{:S(2)}, u32[]{:S(2)}) %collective-permute-start.5) | collective-permute-done | bytes 262176 | tf_op jit(solution)/shard_map/ppermute | solution.py:16
  148.4 1.6 collective-permute-start.8
  150.5 11.1 %collective-permute-done.8 = f32[2,256,256]{1,2,0:T(8,128)S(1)} collective-permute-done((f32[2,256,256]{1,2,0:T(8,128)S(1)}, f32[2,256,256]{1,2,0:T(8,128)S(1)}, u32[]{:S(2)}, u32[]{:S(2)}) %collective-permute-start.8) | collective-permute-done | bytes 524320 | tf_op jit(solution)/shard_map/ppermute | solution.py:99
  161.7 3.1 %collective-permute-start.9 = (f32[2,256,256]{1,2,0:T(8,128)S(1)}, f32[2,256,256]{1,2,0:T(8,128)S(1)}, u32[]{:S(2)}, u32[]{:S(2)}) collective-permute-start(f32[2,256,256]{1,2,0:T(8,128)S(1)} %add.66), channel_id=1, source_target_pairs={{0,128},{64,192},{128,0},{192,64},{1,129},{65,193},{129,1},{193,65... | collective-permute-start | bytes 1572872 | tf_op jit(solution)/shard_map/ppermute | solution.py:99
  167.4 8.3 %collective-permute-done.9 = f32[2,256,256]{1,2,0:T(8,128)S(1)} collective-permute-done((f32[2,256,256]{1,2,0:T(8,128)S(1)}, f32[2,256,256]{1,2,0:T(8,128)S(1)}, u32[]{:S(2)}, u32[]{:S(2)}) %collective-permute-start.9) | collective-permute-done | bytes 524320 | tf_op jit(solution)/shard_map/ppermute | solution.py:99
  176.7 3.5 %all-to-all-start.1 = ((f32[2,256,256]{2,0,1:T(2,128)}), f32[2,256,256]{2,0,1:T(2,128)S(1)}, u32[]{:S(2)}, u32[]{:S(2)}) async-start(f32[2,256,256]{2,0,1:T(2,128)} %copy.191), calls=%async_computation.1 | async-start | bytes 1048576 | tf_op jit(solution)/shard_map/all_to_all | solution.py:100
  180.2 1.6 fusion.41
  182.0 1.4 copy.194
  183.4 5.6 %all-to-all-done.1 = f32[2,256,256]{2,0,1:T(2,128)S(1)} async-done(((f32[2,256,256]{2,0,1:T(2,128)}), f32[2,256,256]{2,0,1:T(2,128)S(1)}, u32[]{:S(2)}, u32[]{:S(2)}) %all-to-all-start.1) | async-done | bytes 524320 | tf_op jit(solution)/shard_map/all_to_all | solution.py:100
  (95 shorter events, 38.9 us)
Async XLA Ops:
  0.6 20.7 %copy-start.9 = (bf16[1,256,2048]{2,1,0:T(8,128)(2,1)S(1)}, bf16[1,256,2048]{2,1,0:T(8,128)(2,1)}, u32[]{:S(2)}) copy-start(bf16[1,256,2048]{2,1,0:T(8,128)(2,1)} %param.4) | copy-start | bytes 3145732
  3.1 9.4 %all-to-all-start = ((bf16[4,2,16384]{2,1,0:T(2,128)(2,1)}), bf16[4,2,16384]{2,1,0:T(2,128)(2,1)S(1)}, u32[]{:S(2)}, u32[]{:S(2)}) async-start(bf16[4,2,16384]{2,1,0:T(2,128)(2,1)} %reshape.105), calls=%async_computation | async-start | bytes 524288 | tf_op jit(solution)/shard_map/all_to_all | solution.py:47
  13.9 24.5 %collective-permute-start = (bf16[2,256,256]{2,1,0:T(8,128)(2,1)}, bf16[2,256,256]{2,1,0:T(8,128)(2,1)}, u32[]{:S(2)}, u32[]{:S(2)}) collective-permute-start(bf16[2,256,256]{2,1,0:T(8,128)(2,1)} %bitcast.2), channel_id=1, source_target_pairs={{0,16},{4,20},{8,24},{12,28},{16,32},{20,36},{24,40},{28,44},{32,4... | collective-permute-start | bytes 786440 | tf_op jit(solution)/shard_map/ppermute | solution.py:16
  21.9 77.7 %copy-start = (bf16[1,256,2048]{1,2,0:T(8,128)(2,1)}, bf16[1,256,2048]{1,2,0:T(8,128)(2,1)S(1)}, u32[]{:S(2)}) copy-start(bf16[1,256,2048]{1,2,0:T(8,128)(2,1)S(1)} %copy.147) | copy-start | bytes 3145732
  21.9 28.7 %collective-permute-start.2 = (bf16[2,256,256]{2,1,0:T(8,128)(2,1)}, bf16[2,256,256]{2,1,0:T(8,128)(2,1)}, u32[]{:S(2)}, u32[]{:S(2)}) collective-permute-start(bf16[2,256,256]{2,1,0:T(8,128)(2,1)} %bitcast.2), channel_id=1, source_target_pairs={{0,8},{4,12},{8,16},{12,20},{16,24},{20,28},{24,32},{28,36},{32,40... | collective-permute-start | bytes 786440 | tf_op jit(solution)/shard_map/ppermute | solution.py:16
  24.8 24.8 %collective-permute-start.1 = (bf16[2,256,256]{2,1,0:T(8,128)(2,1)}, bf16[2,256,256]{2,1,0:T(8,128)(2,1)}, u32[]{:S(2)}, u32[]{:S(2)}) collective-permute-start(bf16[2,256,256]{2,1,0:T(8,128)(2,1)} %bitcast.2), channel_id=1, source_target_pairs={{0,12},{4,16},{8,20},{12,24},{16,28},{20,32},{24,36},{28,40},{32,4... | collective-permute-start | bytes 786440 | tf_op jit(solution)/shard_map/ppermute | solution.py:16
  29.6 59.7 %copy-start.3 = (bf16[1,256,2048]{1,2,0:T(8,128)(2,1)}, bf16[1,256,2048]{1,2,0:T(8,128)(2,1)S(1)}, u32[]{:S(2)}) copy-start(bf16[1,256,2048]{1,2,0:T(8,128)(2,1)S(1)} %copy.145) | copy-start | bytes 3145732
  33.1 20.8 %collective-permute-start.3 = (bf16[2,256,256]{2,1,0:T(8,128)(2,1)}, bf16[2,256,256]{2,1,0:T(8,128)(2,1)S(1)}, u32[]{:S(2)}, u32[]{:S(2)}) collective-permute-start(bf16[2,256,256]{2,1,0:T(8,128)(2,1)} %bitcast.2), channel_id=1, source_target_pairs={{0,4},{4,8},{8,12},{12,16},{16,20},{20,24},{24,28},{28,32},{32,36}... | collective-permute-start | bytes 786440 | tf_op jit(solution)/shard_map/ppermute | solution.py:16
  54.9 43.4 %copy-start.1 = (bf16[2,1280,256]{2,1,0:T(8,128)(2,1)}, bf16[2,1280,256]{2,1,0:T(8,128)(2,1)S(1)}, u32[]{:S(2)}) copy-start(bf16[2,1280,256]{2,1,0:T(8,128)(2,1)S(1)} %constant_dynamic-update-slice_fusion) | copy-start | bytes 3932164
  75.5 6.3 %slice-start.6 = ((s8[5242880]{0:T(1024)(128)(4,1)}), s8[4194304]{0:T(1024)(128)(4,1)S(1)}, s32[]{:S(2)}) async-start(s8[5242880]{0:T(1024)(128)(4,1)} %bitcast.225), calls=%async_computation.8 | async-start | bytes 8388608
  79.4 1.0 copy-start.8
  79.5 2.3 %slice-start.7 = ((s8[5242880]{0:T(1024)(128)(4,1)}), s8[1048576]{0:T(1024)(128)(4,1)S(1)}, s32[]{:S(2)}) async-start(s8[5242880]{0:T(1024)(128)(4,1)} %bitcast.225), calls=%async_computation.9 | async-start | bytes 2097152
  81.7 2.2 %slice-start.4 = ((s8[5242880]{0:T(1024)(128)(4,1)}), s8[4194304]{0:T(1024)(128)(4,1)S(1)}, s32[]{:S(2)}) async-start(s8[5242880]{0:T(1024)(128)(4,1)} %bitcast.223), calls=%async_computation.6 | async-start | bytes 8388608
  81.8 2.5 %slice-start.5 = ((s8[5242880]{0:T(1024)(128)(4,1)}), s8[1048576]{0:T(1024)(128)(4,1)S(1)}, s32[]{:S(2)}) async-start(s8[5242880]{0:T(1024)(128)(4,1)} %bitcast.223), calls=%async_computation.7 | async-start | bytes 2097152
  85.9 1.0 copy-start.7
  88.2 2.2 %slice-start.2 = ((s8[5242880]{0:T(1024)(128)(4,1)}), s8[4194304]{0:T(1024)(128)(4,1)S(1)}, s32[]{:S(2)}) async-start(s8[5242880]{0:T(1024)(128)(4,1)} %bitcast.221), calls=%async_computation.4 | async-start | bytes 8388608
  88.2 2.5 %slice-start.3 = ((s8[5242880]{0:T(1024)(128)(4,1)}), s8[1048576]{0:T(1024)(128)(4,1)S(1)}, s32[]{:S(2)}) async-start(s8[5242880]{0:T(1024)(128)(4,1)} %bitcast.221), calls=%async_computation.5 | async-start | bytes 2097152
  90.6 1.4 copy-start.6
  94.3 2.2 %slice-start = ((s8[5242880]{0:T(1024)(128)(4,1)}), s8[4194304]{0:T(1024)(128)(4,1)S(1)}, s32[]{:S(2)}) async-start(s8[5242880]{0:T(1024)(128)(4,1)} %bitcast.219), calls=%async_computation.2 | async-start | bytes 8388608
  94.4 2.5 %slice-start.1 = ((s8[5242880]{0:T(1024)(128)(4,1)}), s8[1048576]{0:T(1024)(128)(4,1)S(1)}, s32[]{:S(2)}) async-start(s8[5242880]{0:T(1024)(128)(4,1)} %bitcast.219), calls=%async_computation.3 | async-start | bytes 2097152
  96.8 1.4 copy-start.5
  99.6 1.3 copy-start.2
  100.9 2.5 %copy-start.4 = (bf16[1,256,2048]{1,2,0:T(8,128)(2,1)S(1)}, bf16[1,256,2048]{1,2,0:T(8,128)(2,1)}, u32[]{:S(2)}) copy-start(bf16[1,256,2048]{1,2,0:T(8,128)(2,1)} %copy-done.3) | copy-start | bytes 3145732
  105.8 18.1 %collective-permute-start.4 = (bf16[2,256,256]{1,2,0:T(8,128)(2,1)S(1)}, bf16[2,256,256]{1,2,0:T(8,128)(2,1)S(1)}, u32[]{:S(2)}, u32[]{:S(2)}) collective-permute-start(bf16[2,256,256]{1,2,0:T(8,128)(2,1)S(1)} %get-tuple-element.10), channel_id=1, source_target_pairs={{16,0},{20,4},{24,8},{28,12},{32,16},{36,20},{40,24},{44,28},{48,3... | collective-permute-start | bytes 786440 | tf_op jit(solution)/shard_map/ppermute | solution.py:16
  107.8 23.2 %collective-permute-start.7 = (bf16[2,256,256]{1,2,0:T(8,128)(2,1)S(1)}, bf16[2,256,256]{1,2,0:T(8,128)(2,1)S(1)}, u32[]{:S(2)}, u32[]{:S(2)}) collective-permute-start(bf16[2,256,256]{1,2,0:T(8,128)(2,1)S(1)} %get-tuple-element.11), channel_id=1, source_target_pairs={{4,0},{8,4},{12,8},{16,12},{20,16},{24,20},{28,24},{32,28},{36,32}... | collective-permute-start | bytes 786440 | tf_op jit(solution)/shard_map/ppermute | solution.py:16
  111.5 19.4 %collective-permute-start.6 = (bf16[2,256,256]{1,2,0:T(8,128)(2,1)S(1)}, bf16[2,256,256]{1,2,0:T(8,128)(2,1)S(1)}, u32[]{:S(2)}, u32[]{:S(2)}) collective-permute-start(bf16[2,256,256]{1,2,0:T(8,128)(2,1)S(1)} %get-tuple-element.12), channel_id=1, source_target_pairs={{8,0},{12,4},{16,8},{20,12},{24,16},{28,20},{32,24},{36,28},{40,32... | collective-permute-start | bytes 786440 | tf_op jit(solution)/shard_map/ppermute | solution.py:16
  113.5 34.8 %collective-permute-start.5 = (bf16[2,256,256]{1,2,0:T(8,128)(2,1)S(1)}, bf16[2,256,256]{1,2,0:T(8,128)(2,1)S(1)}, u32[]{:S(2)}, u32[]{:S(2)}) collective-permute-start(bf16[2,256,256]{1,2,0:T(8,128)(2,1)S(1)} %get-tuple-element.13), channel_id=1, source_target_pairs={{12,0},{16,4},{20,8},{24,12},{28,16},{32,20},{36,24},{40,28},{44,3... | collective-permute-start | bytes 786440 | tf_op jit(solution)/shard_map/ppermute | solution.py:16
  148.4 13.3 %collective-permute-start.8 = (f32[2,256,256]{1,2,0:T(8,128)S(1)}, f32[2,256,256]{1,2,0:T(8,128)S(1)}, u32[]{:S(2)}, u32[]{:S(2)}) collective-permute-start(f32[2,256,256]{1,2,0:T(8,128)S(1)} %fusion.49), channel_id=1, source_target_pairs={{0,64},{64,0},{128,192},{192,128},{1,65},{65,1},{129,193},{193,129... | collective-permute-start | bytes 1572872 | tf_op jit(solution)/shard_map/ppermute | solution.py:99
  161.7 13.9 %collective-permute-start.9 = (f32[2,256,256]{1,2,0:T(8,128)S(1)}, f32[2,256,256]{1,2,0:T(8,128)S(1)}, u32[]{:S(2)}, u32[]{:S(2)}) collective-permute-start(f32[2,256,256]{1,2,0:T(8,128)S(1)} %add.66), channel_id=1, source_target_pairs={{0,128},{64,192},{128,0},{192,64},{1,129},{65,193},{129,1},{193,65... | collective-permute-start | bytes 1572872 | tf_op jit(solution)/shard_map/ppermute | solution.py:99
  176.7 12.3 %all-to-all-start.1 = ((f32[2,256,256]{2,0,1:T(2,128)}), f32[2,256,256]{2,0,1:T(2,128)S(1)}, u32[]{:S(2)}, u32[]{:S(2)}) async-start(f32[2,256,256]{2,0,1:T(2,128)} %copy.191), calls=%async_computation.1 | async-start | bytes 1048576 | tf_op jit(solution)/shard_map/all_to_all | solution.py:100
  180.2 1.6 copy-start.10
  180.2 1.6 copy-start.11
